TPU v7x, 32 devices: a whole 2x2x4 slice. The times are simulated.
32 devices in a mesh: groups: 2 (over y), ctx: 4 (over z), head: 4 (over x, core).
Axes of the slice: x: 2, y: 2, z: 4, core: 2. Of those that a mesh axis runs over, the one named last changes fastest.
Arguments:
- hidden_in: bfloat16 [2048, 4096], P(('groups', 'ctx'), 'head'), parts along dimension 0, may hold values from -6 to 6
- norm_gain: bfloat16 [4096], P('head'), may hold values from 0.099609375 to 1.8984375
- w_query: bfloat16 [4096, 2048], P('ctx', 'head'), may hold values from -8 to 8
- w_key: bfloat16 [4096, 512], P('ctx', 'head'), may hold values from -8 to 8
- w_value: bfloat16 [4096, 512], P('ctx', 'head'), may hold values from -0.09375 to 0.09375
- w_out: bfloat16 [2048, 4096], P('head', 'ctx'), may hold values from -3 to 3
- session_ids: int32 [2048], P('groups'), parts along dimension 0, may hold values from 0 to 3, never falling along the last dimension, each value on 1 to 512 neighbouring positions
- block_anchor: int32 [16], P('groups'), parts along dimension 0, may hold values from 0 to 7, each once
Outputs:
- block_update: bfloat16 [2048, 4096], P(('groups', 'ctx'), 'head'), parts along dimension 0
There are 2 independent parts, one for each index of `groups`. A program takes and returns all parts, laid end to end along the dimension named above; an argument that names none is the same for every part. Nothing has to cross between parts.
Inputs may be any that keep to these rules, and one draw needn't show every extreme that they name: `session_ids`: session numbers never fall along the contiguous order; 4 sessions, each of 1 to 512 tokens, one of exactly 512. `block_anchor`: each of the 8 blocks appears once.
All inputs are finite; a program needn't handle non-finite values.
Results may differ from a plain program's by a relative error of at most 0.0095.
The roundings to bfloat16 on the way count: a program that leaves them out, or rounds other values in their place, can miss the bound.
Values may be sent and summed in bfloat16 or wider, within the bound.
No kernel may reach another device: no remote copies, remote signals or barrier semaphores. Data moves between devices by JAX's collectives and lax.ppermute only.
A program may use at most 64 MiB of HBM per device.

v0:
```python
import math
import jax
import jax.numpy as jnp
from jax import lax
from jax.sharding import PartitionSpec as P

HD = 128
GROUP = 4
BLOCK = 128
norm_epsilon = 1e-05
rotary_base = 500000.0
masked_score = -1e30


def passed_along(block, axis, distance):
    devices = range(lax.axis_size(axis))
    route = [((i - distance) % len(devices), i) for i in devices]
    return lax.ppermute(block, axis, route)


def session_starts(session_ids):
    length = session_ids.shape[0]
    indices = jnp.arange(length, dtype=jnp.int32)
    fresh = jnp.concatenate([jnp.ones((1,), dtype=jnp.bool_), session_ids[1:] != session_ids[:-1]])
    return lax.cummax(jnp.where(fresh, indices, 0), axis=0)


def rotary(vectors, position):
    half_dim = vectors.shape[-1] // 2
    ladder = jnp.arange(half_dim, dtype=jnp.float32) * (2.0 / vectors.shape[-1])
    frequency = jnp.exp(-ladder * math.log(rotary_base))
    angles = position.astype(jnp.float32).reshape((-1,) + (1,) * (vectors.ndim - 1)) * frequency
    cosine = jnp.cos(angles)
    sines = jnp.sin(angles)
    first_half = vectors[..., :half_dim]
    second_half = vectors[..., half_dim:]
    return jnp.concatenate(
        [first_half * cosine - second_half * sines, second_half * cosine + first_half * sines],
        axis=-1,
    )


def attend_core(
    carry_state, query_heads, query_pos, query_seg, key_heads, value_heads, key_pos, key_seg
):
    row_max, row_sum, mixed_sum = carry_state
    scores = jnp.einsum(
        "qagd,kad->qagk", query_heads, key_heads, preferred_element_type=jnp.float32
    ) * (1.0 / math.sqrt(query_heads.shape[-1]))
    allowed = ((query_seg[:, None] == key_seg[None, :]) & (key_pos[None, :] <= query_pos[:, None]))[
        :, None, None, :
    ]
    new_max = jnp.maximum(row_max, jnp.max(jnp.where(allowed, scores, masked_score), axis=-1))
    weights = jnp.where(allowed, jnp.exp(scores - new_max[..., None]), 0.0)
    rescale = jnp.exp(row_max - new_max)
    row_sum = row_sum * rescale + jnp.sum(weights, axis=-1)
    mixed_sum = mixed_sum * rescale[..., None] + jnp.einsum(
        "qagk,kad->qagd",
        weights.astype(jnp.bfloat16),
        value_heads,
        preferred_element_type=jnp.float32,
    )
    return (new_max, row_sum, mixed_sum)


def per_device_ring(
    hidden_in, norm_gain, w_query, w_key, w_value, w_out, session_ids, block_anchor
):
    whole, gain_full = (
        lax.all_gather(hidden_in, "head", axis=1, tiled=True),
        lax.all_gather(norm_gain, "head", axis=0, tiled=True),
    )
    tok_rows = whole.shape[0]
    cycle_size = lax.axis_size("ctx")
    cycle_index = lax.axis_index("ctx")
    per_shard = tok_rows // BLOCK
    starts = session_starts(session_ids)
    seg_table = session_ids.reshape(-1, BLOCK)
    start_table = starts.reshape(-1, BLOCK)
    offsets = jnp.arange(BLOCK, dtype=jnp.int32)

    def token_info(owner):
        blocks_here = lax.dynamic_slice_in_dim(block_anchor, owner * per_shard, per_shard)
        contiguous = (blocks_here[:, None] * BLOCK + offsets[None, :]).reshape(-1)
        session = jnp.take(seg_table, blocks_here, axis=0).reshape(-1)
        position = contiguous - jnp.take(start_table, blocks_here, axis=0).reshape(-1)
        return (contiguous, session, position)

    wide = whole.astype(jnp.float32)
    normed = (
        wide
        * lax.rsqrt(jnp.mean(wide * wide, axis=-1, keepdims=True) + norm_epsilon)
        * gain_full.astype(jnp.float32)
    ).astype(jnp.bfloat16)
    key_cols = w_key.shape[1]
    kv_local = key_cols // HD
    pieces = (
        lax.all_gather(w_query, "ctx", axis=0, tiled=True),
        lax.all_gather(w_key, "ctx", axis=0, tiled=True),
        lax.all_gather(w_value, "ctx", axis=0, tiled=True),
    )
    query_raw, key_raw, value_raw = tuple(
        (jnp.dot(normed, weight_rows, preferred_element_type=jnp.float32) for weight_rows in pieces)
    )
    my_pos, my_seg, my_place = token_info(cycle_index)
    query_heads = rotary(query_raw.reshape(tok_rows, kv_local, GROUP, HD), my_place).astype(
        jnp.bfloat16
    )
    key_heads = rotary(key_raw.reshape(tok_rows, kv_local, HD), my_place).astype(jnp.bfloat16)
    value_heads = value_raw.astype(jnp.bfloat16).reshape(tok_rows, kv_local, HD)

    def attend(current_state, kv_stack, source):
        key_pos, key_seg, unused_place = token_info(source)
        return attend_core(
            current_state, query_heads, my_pos, my_seg, kv_stack[0], kv_stack[1], key_pos, key_seg
        )

    carry_state = (
        jnp.full((tok_rows, kv_local, GROUP), masked_score, jnp.float32),
        jnp.zeros((tok_rows, kv_local, GROUP), jnp.float32),
        jnp.zeros((tok_rows, kv_local, GROUP, HD), jnp.float32),
    )
    own_stack = jnp.stack([key_heads, value_heads])
    carry_state = attend(carry_state, own_stack, cycle_index)

    def cycle_turn(turn_index, loop_carry):
        current_state, moving = loop_carry
        moving = passed_along(moving, "ctx", 1)
        current_state = attend(current_state, moving, (cycle_index - turn_index) % cycle_size)
        return (current_state, moving)

    carry_state, unused_stack = lax.fori_loop(1, cycle_size, cycle_turn, (carry_state, own_stack))
    final_max, row_sum, mixed_sum = carry_state
    attended = (mixed_sum / row_sum[..., None]).astype(jnp.bfloat16).reshape(tok_rows, -1)
    terms = jnp.dot(
        attended,
        lax.all_gather(w_out, "ctx", axis=1, tiled=True),
        preferred_element_type=jnp.float32,
    )
    return lax.psum_scatter(terms.astype(jnp.bfloat16), "head", scatter_dimension=1, tiled=True)


def token_table(session_ids, block_anchor, owners_rows):
    starts = session_starts(session_ids)
    owner = jnp.arange(owners_rows, dtype=jnp.int32)
    contiguous = jnp.take(block_anchor, owner // BLOCK) * BLOCK + owner % BLOCK
    session = jnp.take(session_ids, contiguous)
    position = contiguous - jnp.take(starts, contiguous)
    return (contiguous, session, position)


def transposed(block, n):
    route = [(c * n + h, h * n + c) for c in range(n) for h in range(n)]
    return lax.ppermute(block, ("ctx", "head"), route)


def per_device_ws(hidden_in, norm_gain, w_query, w_key, w_value, w_out, session_ids, block_anchor):
    n = lax.axis_size("ctx")
    cycle_index = lax.axis_index("ctx")
    tok_rows, local_feats = hidden_in.shape
    wide = hidden_in.astype(jnp.float32)
    squares = lax.psum(jnp.sum(wide * wide, axis=-1, keepdims=True), "head")
    normed = (
        wide * lax.rsqrt(squares / (local_feats * n) + norm_epsilon) * norm_gain.astype(jnp.float32)
    ).astype(jnp.bfloat16)
    every = lax.all_gather(transposed(normed, n), "head", axis=0, tiled=True)
    q_cols, k_cols = (w_query.shape[1], w_key.shape[1])
    stacked = jnp.concatenate([w_query, w_key, w_value], axis=1)
    partial = jnp.dot(every, stacked, preferred_element_type=jnp.float32)
    mine = lax.psum_scatter(partial, "ctx", scatter_dimension=0, tiled=True)
    kv_local = k_cols // HD
    query_raw = mine[:, :q_cols].reshape(tok_rows, kv_local, GROUP, HD)
    key_raw = mine[:, q_cols : q_cols + k_cols].reshape(tok_rows, kv_local, HD)
    value_raw = mine[:, q_cols + k_cols :].reshape(tok_rows, kv_local, HD)
    contiguous, session, position = token_table(session_ids, block_anchor, tok_rows * n)
    my_pos = lax.dynamic_slice_in_dim(contiguous, cycle_index * tok_rows, tok_rows)
    my_seg = lax.dynamic_slice_in_dim(session, cycle_index * tok_rows, tok_rows)
    my_place = lax.dynamic_slice_in_dim(position, cycle_index * tok_rows, tok_rows)
    query_heads = rotary(query_raw, my_place).astype(jnp.bfloat16)
    key_heads = rotary(key_raw, my_place).astype(jnp.bfloat16)
    value_heads = value_raw.astype(jnp.bfloat16)
    kv_all = lax.all_gather(jnp.stack([key_heads, value_heads]), "ctx", axis=1, tiled=True)
    scores = jnp.einsum(
        "qagd,kad->qagk", query_heads, kv_all[0], preferred_element_type=jnp.float32
    ) * (1.0 / math.sqrt(HD))
    allowed = ((my_seg[:, None] == session[None, :]) & (contiguous[None, :] <= my_pos[:, None]))[
        :, None, None, :
    ]
    row_max = jnp.max(jnp.where(allowed, scores, masked_score), axis=-1, keepdims=True)
    weights = jnp.where(allowed, jnp.exp(scores - row_max), 0.0)
    row_sum = jnp.sum(weights, axis=-1, keepdims=True)
    mixed = jnp.einsum(
        "qagk,kad->qagd",
        weights.astype(jnp.bfloat16),
        kv_all[1],
        preferred_element_type=jnp.float32,
    )
    attended = (mixed / row_sum).astype(jnp.bfloat16).reshape(tok_rows, -1)
    att_all = lax.all_gather(attended, "ctx", axis=0, tiled=True)
    terms = jnp.dot(att_all, w_out, preferred_element_type=jnp.float32).astype(jnp.bfloat16)
    summed = lax.psum_scatter(terms, "head", scatter_dimension=0, tiled=True)
    return transposed(summed, n)


def solution(mesh):
    in_specs = (
        P(("groups", "ctx"), "head"),
        P("head"),
        P("ctx", "head"),
        P("ctx", "head"),
        P("ctx", "head"),
        P("head", "ctx"),
        P("groups"),
        P("groups"),
    )
    out_specs = P(("groups", "ctx"), "head")
    square = mesh.shape["ctx"] == mesh.shape["head"]
    per_device = per_device_ws if square else per_device_ring
    return jax.shard_map(
        per_device, mesh=mesh, in_specs=in_specs, out_specs=out_specs, check_vma=False
    )
```

profile of v0, /device:TPU:2, one launch (start us, length us, event | category | flops | bytes accessed | tf_op | source)
XLA Modules:
  0.0 255.6 jit_solution(16360974636456427770)
XLA Ops:
  6.5 0.0 copy-start
  6.5 0.0 all-gather.3.cloned.1.call-start
  6.5 0.8 convert_element_type.42
  7.3 1.2 fusion.18
  8.5 5.8 %psum.7 = f32[256,1]{0,1:T(1,128)S(1)} all-reduce(f32[256,1]{0,1:T(1,128)S(1)} %bitcast.89), channel_id=1, replica_groups=mesh['groups'=2,'ctx'=4,'head'=4] {'head'}, use_global_device_ids=true, to_apply=%region_1.0 | all-reduce | flops 256 | bytes 2048 | tf_op jit(solution)/shard_map/psum | solution.py:162
  14.3 1.2 fusion.20
  15.5 5.6 %collective-permute-start = (bf16[256,1024]{1,0:T(8,128)(2,1)S(1)}, bf16[256,1024]{1,0:T(8,128)(2,1)S(1)}, u32[]{:S(2)}, u32[]{:S(2)}) collective-permute-start(bf16[256,1024]{1,0:T(8,128)(2,1)S(1)} %fusion.20), channel_id=1, source_target_pairs={{0,0},{1,4},{2,8},{3,12},{4,1},{5,5},{6,9},{7,13},{8,2},{9,6},{10,... | collective-permute-start | bytes 1572872 | tf_op jit(solution)/shard_map/ppermute | solution.py:154
  21.2 23.8 %collective-permute-done = bf16[256,1024]{1,0:T(8,128)(2,1)S(1)} collective-permute-done((bf16[256,1024]{1,0:T(8,128)(2,1)S(1)}, bf16[256,1024]{1,0:T(8,128)(2,1)S(1)}, u32[]{:S(2)}, u32[]{:S(2)}) %collective-permute-start) | collective-permute-done | bytes 524320 | tf_op jit(solution)/shard_map/ppermute | solution.py:154
  45.0 0.0 copy-start.2
  45.0 0.8 copy-done.2
  45.7 0.0 all-gather.3.cloned.1.call-update
  45.8 0.0 copy-start.1
  45.8 0.0 copy-start.3
  45.8 0.0 reduce-scatter.3.cloned.1.call-start
  45.8 20.0 %all-gather.3.cloned.1.call-done = bf16[1024,1024]{1,0:T(8,128)(2,1)} async-done(((bf16[256,1024]{1,0:T(8,128)(2,1)}), bf16[1024,1024]{1,0:T(8,128)(2,1)}) %all-gather.3.cloned.1.call-update) | async-done | bytes 2097168 | tf_op jit(solution)/shard_map/all_gather | solution.py:166
  65.8 5.5 %fusion.9 = f32[1024,768]{1,0:T(8,128)} fusion(bf16[1024,1024]{1,0:T(8,128)(2,1)} %all-gather.3.cloned.1.call-done, bf16[1024,128]{1,0:T(8,128)(2,1)} %param.14, bf16[1024,128]{1,0:T(8,128)(2,1)} %param.13, bf16[1024,512]{1,0:T(8,128)(2,1)} %param.12), kind=kOutput, calls=%fused_computation.13 | convolution fusion | flops 1615331328 | bytes 6815744 | tf_op jit(solution)/shard_map/dot_general | solution.py:169
  71.3 0.0 reduce-scatter.3.cloned.1.call-update
  71.3 0.0 all-gather.5.cloned.1.call-start
  71.4 0.0 copy-done.1
  71.4 0.1 slice_compare_fusion
  71.4 0.1 add_select_fusion.1
  71.5 0.3 reduce-window.9
  71.8 0.1 slice.45
  71.9 0.0 copy-done.3
  71.9 0.7 fusion.63
  72.6 4.3 %compare_select_fusion.1 = s32[1024,1]{0,1:T(1,128)S(1)} fusion(s32[]{:T(128)} %bitcast.4, s32[]{:T(128)} %bitcast.5, s32[]{:T(128)} %bitcast.6, s32[]{:T(128)} %bitcast.7, s32[]{:T(128)} %bitcast.8, s32[]{:T(128)} %bitcast.10, s32[]{:T(128)} %bitcast.9), kind=kLoop, calls=%fused_computation.58 | loop fusion | flops 23552 | bytes 4124 | tf_op jit(solution)/shard_map/jit(_take)/gather | solution.py:146
  77.0 0.7 fusion.56
  77.6 4.5 %gather_fusion.1 = s32[1024]{0:T(1024)S(1)} fusion(s32[1024]{0:T(1024)S(1)} %copy-done.1, s32[1024]{0:T(1024)S(1)} %get-tuple-element.6), kind=kCustom, calls=%fused_computation.1.clone | custom fusion | bytes 12288 | tf_op jit(solution)/shard_map/jit(_take)/gather | solution.py:147
  82.2 0.1 slice_reduce_fusion
  82.3 0.1 maximum_bitcast_fusion
  82.4 4.5 %gather_fusion = s32[1024]{0:T(1024)S(1)} fusion(s32[1024]{0:T(1024)S(1)} %maximum_bitcast_fusion, s32[1024]{0:T(1024)S(1)} %get-tuple-element.6), kind=kCustom, calls=%fused_computation.clone | custom fusion | bytes 12288 | tf_op jit(solution)/shard_map/jit(_take)/gather | solution.py:148
  86.9 0.1 dynamic_slice.11
  87.0 0.1 dynamic_slice.10
  87.1 0.1 dynamic-slice_convert_fusion
  87.1 0.5 multiply_cosine_fusion
  87.7 0.3 compare_and_fusion
  88.0 45.0 %reduce-scatter.3.cloned.1.call-done = f32[256,768]{1,0:T(8,128)} async-done(((f32[1024,768]{1,0:T(8,128)}), f32[256,768]{1,0:T(8,128)}) %reduce-scatter.3.cloned.1.call-update) | async-done | bytes 786448 | tf_op jit(solution)/shard_map/reduce_scatter | solution.py:170
  133.0 0.9 slice_bitcast_fusion.4
  133.9 0.6 fusion.43
  134.5 0.9 fusion.41
  135.4 0.1 pad_maximum_fusion
  135.5 15.2 %all_gather.10 = bf16[2,1024,1,128]{3,1,2,0:T(8,128)(2,1)S(1)} all-gather(bf16[2,256,1,128]{3,1,2,0:T(8,128)(2,1)S(1)} %pad_maximum_fusion), channel_id=1, replica_groups=mesh['groups'=2,'ctx'=4,'head'=4] {'ctx'}, dimensions={1}, use_global_device_ids=true | all-gather | bytes 655360 | tf_op jit(solution)/shard_map/all_gather | solution.py:182
  150.8 1.1 slice.74
  151.8 0.2 reshape.406
  152.0 0.3 fusion.62
  152.4 0.1 fusion.27
  152.5 0.9 fusion
  153.4 0.9 fusion.3
  154.3 1.7 fusion.24
  156.1 0.0 all-gather.5.cloned.1.call-update
  156.1 0.0 reduce-scatter.5.cloned.1.call-start
  156.2 29.4 %all-gather.5.cloned.1.call-done = bf16[1024,512]{0,1:T(8,128)(2,1)} async-done(((bf16[256,512]{0,1:T(8,128)(2,1)}), bf16[1024,512]{0,1:T(8,128)(2,1)}) %all-gather.5.cloned.1.call-update) | async-done | bytes 1048592 | tf_op jit(solution)/shard_map/all_gather | solution.py:199
  185.5 0.0 copy-done
  185.6 3.9 %convolution_convert_fusion = bf16[1024,1024]{1,0:T(8,128)(2,1)} fusion(bf16[1024,512]{0,1:T(8,128)(2,1)} %all-gather.5.cloned.1.call-done, bf16[512,1024]{1,0:T(8,128)(2,1)S(1)} %copy-done), kind=kOutput, calls=%fused_computation.12 | convolution fusion | flops 1074790400 | bytes 4194304 | tf_op jit(solution)/shard_map/dot_general | solution.py:200
  189.4 0.0 reduce-scatter.5.cloned.1.call-update
  189.4 29.3 %reduce-scatter.5.cloned.1.call-done = bf16[256,1024]{1,0:T(8,128)(2,1)} async-done(((bf16[1024,1024]{1,0:T(8,128)(2,1)}), bf16[256,1024]{1,0:T(8,128)(2,1)}) %reduce-scatter.5.cloned.1.call-update) | async-done | bytes 524304 | tf_op jit(solution)/shard_map/reduce_scatter | solution.py:201
  218.7 5.4 %collective-permute-start.1 = (bf16[256,1024]{1,0:T(8,128)(2,1)}, bf16[256,1024]{1,0:T(8,128)(2,1)S(1)}, u32[]{:S(2)}, u32[]{:S(2)}) collective-permute-start(bf16[256,1024]{1,0:T(8,128)(2,1)} %reduce-scatter.5.cloned.1.call-done), channel_id=1, source_target_pairs={{0,0},{1,4},{2,8},{3,12},{4,1},{5,5},{6,9},{7,13},{8,2},{9,6},{10,... | collective-permute-start | bytes 1572872 | tf_op jit(solution)/shard_map/ppermute | solution.py:154
  224.1 24.2 %collective-permute-done.1 = bf16[256,1024]{1,0:T(8,128)(2,1)S(1)} collective-permute-done((bf16[256,1024]{1,0:T(8,128)(2,1)}, bf16[256,1024]{1,0:T(8,128)(2,1)S(1)}, u32[]{:S(2)}, u32[]{:S(2)}) %collective-permute-start.1) | collective-permute-done | bytes 524320 | tf_op jit(solution)/shard_map/ppermute | solution.py:154
  248.3 0.8 copy.35
  (5 shorter events, 0.1 us)
Async XLA Ops:
  6.5 179.0 %copy-start = (bf16[512,1024]{1,0:T(8,128)(2,1)S(1)}, bf16[512,1024]{1,0:T(8,128)(2,1)}, u32[]{:S(2)}) copy-start(bf16[512,1024]{1,0:T(8,128)(2,1)} %param.15) | copy-start | bytes 3145732
  6.5 59.3 %all-gather.3.cloned.1.call-start = ((), (), s32[]{:S(2)}) async-start(), calls=%async_computation.2 | async-start | bytes 2621440 | tf_op jit(solution)/shard_map/all_gather | solution.py:166
  15.5 29.4 %collective-permute-start = (bf16[256,1024]{1,0:T(8,128)(2,1)S(1)}, bf16[256,1024]{1,0:T(8,128)(2,1)S(1)}, u32[]{:S(2)}, u32[]{:S(2)}) collective-permute-start(bf16[256,1024]{1,0:T(8,128)(2,1)S(1)} %fusion.20), channel_id=1, source_target_pairs={{0,0},{1,4},{2,8},{3,12},{4,1},{5,5},{6,9},{7,13},{8,2},{9,6},{10,... | collective-permute-start | bytes 1572872 | tf_op jit(solution)/shard_map/ppermute | solution.py:154
  45.0 0.8 copy-start.2
  45.8 25.6 %copy-start.1 = (s32[1024]{0:T(1024)S(1)}, s32[1024]{0:T(1024)}, u32[]{:S(2)}) copy-start(s32[1024]{0:T(1024)} %param.16) | copy-start | bytes 12292
  45.8 26.2 %copy-start.3 = (s32[8]{0:T(128)S(1)}, s32[8]{0:T(128)}, u32[]{:S(2)}) copy-start(s32[8]{0:T(128)} %param.17) | copy-start | bytes 100
  45.8 87.2 %reduce-scatter.3.cloned.1.call-start = ((), (), s32[]{:S(2)}) async-start(), calls=%async_computation.3 | async-start | bytes 3932160 | tf_op jit(solution)/shard_map/reduce_scatter | solution.py:170
  71.3 114.2 %all-gather.5.cloned.1.call-start = ((), (), s32[]{:S(2)}) async-start(), calls=%async_computation.4 | async-start | bytes 1310720 | tf_op jit(solution)/shard_map/all_gather | solution.py:199
  156.1 62.6 %reduce-scatter.5.cloned.1.call-start = ((), (), s32[]{:S(2)}) async-start(), calls=%async_computation.5 | async-start | bytes 2621440 | tf_op jit(solution)/shard_map/reduce_scatter | solution.py:201
  218.7 29.6 %collective-permute-start.1 = (bf16[256,1024]{1,0:T(8,128)(2,1)}, bf16[256,1024]{1,0:T(8,128)(2,1)S(1)}, u32[]{:S(2)}, u32[]{:S(2)}) collective-permute-start(bf16[256,1024]{1,0:T(8,128)(2,1)} %reduce-scatter.5.cloned.1.call-done), channel_id=1, source_target_pairs={{0,0},{1,4},{2,8},{3,12},{4,1},{5,5},{6,9},{7,13},{8,2},{9,6},{10,... | collective-permute-start | bytes 1572872 | tf_op jit(solution)/shard_map/ppermute | solution.py:154
Sparse Core Ops, SparseCore 0:
  45.9 19.8 all-gather.2
  71.4 61.5 reduce-scatter.2
  156.2 29.2 all-gather.4
  189.6 29.1 reduce-scatter.4
where the time goes:
time: 256 us
  waiting for transfers between devices  172 us (67%)
  blocking collectives  21 us (8%)
  local copies, waits for them, and re-layouts  15.1 us (6%)
  between operations  13.3 us (5%)
  matrix products  12 us (5%)
  other arithmetic  11.5 us (4%)
  starting transfers between devices  11.1 us (4%)
    ppermute x2, waiting for transfers between devices, transposed(): return lax.ppermute(block, ('ctx', 'head'), route)  48 us
    reduce_scatter x1, waiting for transfers between devices, per_device_ws(): mine = lax.psum_scatter(partial, 'ctx', scatter_dimension=0, tiled=True)  45 us
    all_gather x1, waiting for transfers between devices, per_device_ws(): att_all = lax.all_gather(attended, 'ctx', axis=0, tiled=True)  29.4 us
    reduce_scatter x1, waiting for transfers between devices, per_device_ws(): summed = lax.psum_scatter(terms, 'head', scatter_dimension=0, tiled=True)  29.3 us
    all_gather x1, waiting for transfers between devices, per_device_ws(): every = lax.all_gather(transposed(normed, n), 'head', axis=0, tiled=True)  20 us
    all_gather x1, blocking collectives, per_device_ws(): lax.all_gather(jnp.stack([key_heads, value_heads]), 'ctx', axis=1, tiled=...  15.2 us
    ppermute x2, starting transfers between devices, transposed(): return lax.ppermute(block, ('ctx', 'head'), route)  11 us
    psum x1, blocking collectives, per_device_ws(): squares = lax.psum(jnp.sum(wide * wide, axis=-1, keepdims=True), 'head')  5.77 us
  transfers between devices with their start and end apart: 6, of which 6 were waited for; matrix products, arithmetic and copies ran while one was open for 6% of the time, Pallas kernels for 0%

commit v1 on v0

--- a/solution.py
+++ b/solution.py
@@ -10,6 +10,28 @@
 norm_epsilon = 1e-05
 rotary_base = 500000.0
 masked_score = -1e30
+
+
+def in_order(parts, dim):
+    shape = list(parts.shape[1:])
+    shape[dim] *= parts.shape[0]
+    return jnp.moveaxis(parts, 0, dim).reshape(shape)
+
+
+def ring_gather(x, axis, dim):
+    count = lax.axis_size(axis)
+    pairs = [(i, (i + 1) % count) for i in range(count)]
+    back = [(b, a) for a, b in pairs]
+    lower, upper = ([], [])
+    for hop in range(count - 1):
+        if hop % 2 == 0:
+            lower.append(lax.ppermute(lower[-1] if lower else x, axis, pairs))
+        else:
+            upper.append(lax.ppermute(upper[-1] if upper else x, axis, back))
+    parts = jnp.stack([*lower[::-1], x, *upper])
+    shift = lax.axis_index(axis) - len(lower)
+    parts = parts[(jnp.arange(count) - shift) % count]
+    return in_order(parts, dim)
 
 
 def passed_along(block, axis, distance):
@@ -163,7 +185,7 @@
     normed = (
         wide * lax.rsqrt(squares / (local_feats * n) + norm_epsilon) * norm_gain.astype(jnp.float32)
     ).astype(jnp.bfloat16)
-    every = lax.all_gather(transposed(normed, n), "head", axis=0, tiled=True)
+    every = ring_gather(transposed(normed, n), "head", 0)
     q_cols, k_cols = (w_query.shape[1], w_key.shape[1])
     stacked = jnp.concatenate([w_query, w_key, w_value], axis=1)
     partial = jnp.dot(every, stacked, preferred_element_type=jnp.float32)

time: 256 us -> 258 us (level)
  waiting for transfers between devices: 172 us -> 169 us
    all_gather x1 -> x0, waiting for transfers between devices: 20 us -> none  [per_device_ws(): every = lax.all_gather(transposed(normed, n), 'head', axis=0, tiled=True)]
    ppermute x0 -> x3, waiting for transfers between devices: none -> 15.4 us  [the longest x2 10.5 us: ring_gather(): lower.append(lax.ppermute(lower[-1] if lower else x, axis, pairs))]
  transfers between devices with their start and end apart: 6 -> 8, of which waited for: 6 -> 8; matrix products, arithmetic and copies ran while one was open for 6% -> 6% of each run, Pallas kernels for 0% -> 0%
where the time goes in v1:
time: 258 us
  waiting for transfers between devices  169 us (66%)
  blocking collectives  21 us (8%)
  local copies, waits for them, and re-layouts  16.7 us (6%)
  other arithmetic  13.3 us (5%)
  between operations  13.3 us (5%)
  starting transfers between devices  12.8 us (5%)
  matrix products  11.9 us (5%)
    ppermute x2, waiting for transfers between devices, transposed(): return lax.ppermute(block, ('ctx', 'head'), route)  48.1 us
    reduce_scatter x1, waiting for transfers between devices, per_device_ws(): mine = lax.psum_scatter(partial, 'ctx', scatter_dimension=0, tiled=True)  46.3 us
    all_gather x1, waiting for transfers between devices, per_device_ws(): att_all = lax.all_gather(attended, 'ctx', axis=0, tiled=True)  29.4 us
    reduce_scatter x1, waiting for transfers between devices, per_device_ws(): summed = lax.psum_scatter(terms, 'head', scatter_dimension=0, tiled=True)  29.3 us
    all_gather x1, blocking collectives, per_device_ws(): lax.all_gather(jnp.stack([key_heads, value_heads]), 'ctx', axis=1, tiled=...  15.3 us
    ppermute x2, starting transfers between devices, transposed(): return lax.ppermute(block, ('ctx', 'head'), route)  11 us
    ppermute x2, waiting for transfers between devices, ring_gather(): lower.append(lax.ppermute(lower[-1] if lower else x, axis, pairs))  10.5 us
    psum x1, blocking collectives, per_device_ws(): squares = lax.psum(jnp.sum(wide * wide, axis=-1, keepdims=True), 'head')  5.77 us
  transfers between devices with their start and end apart: 8, of which 8 were waited for; matrix products, arithmetic and copies ran while one was open for 6% of the time, Pallas kernels for 0%

profile of v1, /device:TPU:2, one launch (start us, length us, event | category | flops | bytes accessed | tf_op | source)
XLA Modules:
  0.0 257.5 jit_solution(3044271662013856566)
XLA Ops:
  6.5 0.0 copy-start
  6.5 0.0 reduce-scatter.3.cloned.1.call-start
  6.5 0.8 convert_element_type.42
  7.3 1.2 fusion.18
  8.5 5.8 %psum.7 = f32[256,1]{0,1:T(1,128)S(1)} all-reduce(f32[256,1]{0,1:T(1,128)S(1)} %bitcast.101), channel_id=1, replica_groups=mesh['groups'=2,'ctx'=4,'head'=4] {'head'}, use_global_device_ids=true, to_apply=%region_1.0 | all-reduce | flops 256 | bytes 2048 | tf_op jit(solution)/shard_map/psum | solution.py:184
  14.3 1.2 fusion.20
  15.5 5.6 %collective-permute-start = (bf16[256,1024]{1,0:T(8,128)(2,1)S(1)}, bf16[256,1024]{1,0:T(8,128)(2,1)S(1)}, u32[]{:S(2)}, u32[]{:S(2)}) collective-permute-start(bf16[256,1024]{1,0:T(8,128)(2,1)S(1)} %fusion.20), channel_id=1, source_target_pairs={{0,0},{1,4},{2,8},{3,12},{4,1},{5,5},{6,9},{7,13},{8,2},{9,6},{10,... | collective-permute-start | bytes 1572872 | tf_op jit(solution)/shard_map/ppermute | solution.py:176
  21.2 23.9 %collective-permute-done = bf16[256,1024]{1,0:T(8,128)(2,1)S(1)} collective-permute-done((bf16[256,1024]{1,0:T(8,128)(2,1)S(1)}, bf16[256,1024]{1,0:T(8,128)(2,1)S(1)}, u32[]{:S(2)}, u32[]{:S(2)}) %collective-permute-start) | collective-permute-done | bytes 524320 | tf_op jit(solution)/shard_map/ppermute | solution.py:176
  45.1 0.0 collective-permute-start.1
  45.1 1.7 collective-permute-start.3
  46.8 6.9 %collective-permute-done.1 = bf16[256,1024]{1,0:T(8,128)(2,1)S(1)} collective-permute-done((bf16[256,1024]{1,0:T(8,128)(2,1)S(1)}, bf16[256,1024]{1,0:T(8,128)(2,1)S(1)}, u32[]{:S(2)}, u32[]{:S(2)}) %collective-permute-start.1) | collective-permute-done | bytes 524320 | tf_op jit(solution)/shard_map/ppermute | solution.py:28
  53.7 0.0 collective-permute-start.2
  53.7 4.9 %collective-permute-done.3 = bf16[256,1024]{1,0:T(8,128)(2,1)S(1)} collective-permute-done((bf16[256,1024]{1,0:T(8,128)(2,1)S(1)}, bf16[256,1024]{1,0:T(8,128)(2,1)S(1)}, u32[]{:S(2)}, u32[]{:S(2)}) %collective-permute-start.3) | collective-permute-done | bytes 524320 | tf_op jit(solution)/shard_map/ppermute | solution.py:30
  58.6 3.7 %collective-permute-done.2 = bf16[256,1024]{1,0:T(8,128)(2,1)S(1)} collective-permute-done((bf16[256,1024]{1,0:T(8,128)(2,1)S(1)}, bf16[256,1024]{1,0:T(8,128)(2,1)S(1)}, u32[]{:S(2)}, u32[]{:S(2)}) %collective-permute-start.2) | collective-permute-done | bytes 524320 | tf_op jit(solution)/shard_map/ppermute | solution.py:28
  62.3 0.0 copy-done.2
  62.3 0.0 copy-done.3
  62.3 0.0 copy-done.4
  62.3 0.8 copy-done.5
  63.1 1.8 pad_maximum_fusion
  64.8 0.0 copy-start.7
  64.9 2.0 gather_fusion
  66.9 0.0 copy-done.7
  66.9 5.4 %fusion.9 = f32[1024,768]{1,0:T(8,128)} fusion(bf16[1024,1024]{1,0:T(8,128)(2,1)} %bitcast.93, bf16[1024,128]{1,0:T(8,128)(2,1)S(1)} %copy-done.7, bf16[1024,128]{1,0:T(8,128)(2,1)} %param.13, bf16[1024,512]{1,0:T(8,128)(2,1)} %param.12), kind=kOutput, calls=%fused_computation.15 | convolution fusion | flops 1615331328 | bytes 6815744 | tf_op jit(solution)/shard_map/dot_general | solution.py:191
  72.3 0.0 reduce-scatter.3.cloned.1.call-update
  72.3 0.0 all-gather.2.cloned.1.call-start
  72.4 0.6 copy-done.1
  73.0 0.1 slice_compare_fusion
  73.0 0.1 add_select_fusion.1
  73.1 0.3 reduce-window.9
  73.4 0.1 slice.45
  73.5 0.0 copy-done.6
  73.5 0.7 fusion.65
  74.2 4.3 %compare_select_fusion.1 = s32[1024,1]{0,1:T(1,128)S(1)} fusion(s32[]{:T(128)} %bitcast.10, s32[]{:T(128)} %bitcast.11, s32[]{:T(128)} %bitcast.12, s32[]{:T(128)} %bitcast.13, s32[]{:T(128)} %bitcast.14, s32[]{:T(128)} %bitcast.16, s32[]{:T(128)} %bitcast.15), kind=kLoop, calls=%fused_computation.60 | loop fusion | flops 23552 | bytes 4124 | tf_op jit(solution)/shard_map/jit(_take)/gather | solution.py:168
  78.6 0.7 fusion.56
  79.2 4.5 %gather_fusion.2 = s32[1024]{0:T(1024)S(1)} fusion(s32[1024]{0:T(1024)S(1)} %copy-done.1, s32[1024]{0:T(1024)S(1)} %get-tuple-element.6), kind=kCustom, calls=%fused_computation.1.clone | custom fusion | bytes 12288 | tf_op jit(solution)/shard_map/jit(_take)/gather | solution.py:169
  83.8 0.1 slice_reduce_fusion
  83.9 0.1 maximum_bitcast_fusion
  84.0 4.5 %gather_fusion.1 = s32[1024]{0:T(1024)S(1)} fusion(s32[1024]{0:T(1024)S(1)} %maximum_bitcast_fusion, s32[1024]{0:T(1024)S(1)} %get-tuple-element.6), kind=kCustom, calls=%fused_computation.clone | custom fusion | bytes 12288 | tf_op jit(solution)/shard_map/jit(_take)/gather | solution.py:170
  88.5 0.1 dynamic_slice.11
  88.6 0.1 dynamic_slice.10
  88.7 0.1 dynamic-slice_convert_fusion
  88.8 0.5 multiply_cosine_fusion
  89.3 0.3 compare_and_fusion
  89.6 46.3 %reduce-scatter.3.cloned.1.call-done = f32[256,768]{1,0:T(8,128)} async-done(((f32[1024,768]{1,0:T(8,128)}), f32[256,768]{1,0:T(8,128)}) %reduce-scatter.3.cloned.1.call-update) | async-done | bytes 786448 | tf_op jit(solution)/shard_map/reduce_scatter | solution.py:192
  135.9 1.0 slice_bitcast_fusion.4
  136.9 0.6 fusion.43
  137.5 0.9 fusion.41
  138.4 0.1 pad_maximum_fusion.1
  138.5 15.3 %all_gather.6 = bf16[2,1024,1,128]{3,1,2,0:T(8,128)(2,1)S(1)} all-gather(bf16[2,256,1,128]{3,1,2,0:T(8,128)(2,1)S(1)} %pad_maximum_fusion.1), channel_id=1, replica_groups=mesh['groups'=2,'ctx'=4,'head'=4] {'ctx'}, dimensions={1}, use_global_device_ids=true | all-gather | bytes 655360 | tf_op jit(solution)/shard_map/all_gather | solution.py:204
  153.8 0.2 reshape.459
  154.0 0.3 fusion.64
  154.3 0.1 fusion.27
  154.4 0.9 fusion
  155.3 0.9 fusion.3
  156.2 1.7 fusion.24
  158.0 0.0 all-gather.2.cloned.1.call-update
  158.0 0.0 reduce-scatter.5.cloned.1.call-start
  158.1 29.4 %all-gather.2.cloned.1.call-done = bf16[1024,512]{0,1:T(8,128)(2,1)} async-done(((bf16[256,512]{0,1:T(8,128)(2,1)}), bf16[1024,512]{0,1:T(8,128)(2,1)}) %all-gather.2.cloned.1.call-update) | async-done | bytes 1048592 | tf_op jit(solution)/shard_map/all_gather | solution.py:221
  187.5 3.9 %convolution_convert_fusion = bf16[1024,1024]{1,0:T(8,128)(2,1)} fusion(bf16[1024,512]{0,1:T(8,128)(2,1)} %all-gather.2.cloned.1.call-done, bf16[512,1024]{1,0:T(8,128)(2,1)S(1)} %copy-done), kind=kOutput, calls=%fused_computation.14 | convolution fusion | flops 1074790400 | bytes 4194304 | tf_op jit(solution)/shard_map/dot_general | solution.py:222
  191.3 0.0 reduce-scatter.5.cloned.1.call-update
  191.3 29.3 %reduce-scatter.5.cloned.1.call-done = bf16[256,1024]{1,0:T(8,128)(2,1)} async-done(((bf16[1024,1024]{1,0:T(8,128)(2,1)}), bf16[256,1024]{1,0:T(8,128)(2,1)}) %reduce-scatter.5.cloned.1.call-update) | async-done | bytes 524304 | tf_op jit(solution)/shard_map/reduce_scatter | solution.py:223
  220.6 5.4 %collective-permute-start.4 = (bf16[256,1024]{1,0:T(8,128)(2,1)}, bf16[256,1024]{1,0:T(8,128)(2,1)S(1)}, u32[]{:S(2)}, u32[]{:S(2)}) collective-permute-start(bf16[256,1024]{1,0:T(8,128)(2,1)} %reduce-scatter.5.cloned.1.call-done), channel_id=1, source_target_pairs={{0,0},{1,4},{2,8},{3,12},{4,1},{5,5},{6,9},{7,13},{8,2},{9,6},{10,... | collective-permute-start | bytes 1572872 | tf_op jit(solution)/shard_map/ppermute | solution.py:176
  226.1 24.2 %collective-permute-done.4 = bf16[256,1024]{1,0:T(8,128)(2,1)S(1)} collective-permute-done((bf16[256,1024]{1,0:T(8,128)(2,1)}, bf16[256,1024]{1,0:T(8,128)(2,1)S(1)}, u32[]{:S(2)}, u32[]{:S(2)}) %collective-permute-start.4) | collective-permute-done | bytes 524320 | tf_op jit(solution)/shard_map/ppermute | solution.py:176
  250.2 0.8 copy.35
  (16 shorter events, 0.1 us)
Async XLA Ops:
  6.5 180.9 %copy-start = (bf16[512,1024]{1,0:T(8,128)(2,1)S(1)}, bf16[512,1024]{1,0:T(8,128)(2,1)}, u32[]{:S(2)}) copy-start(bf16[512,1024]{1,0:T(8,128)(2,1)} %param.15) | copy-start | bytes 3145732
  6.5 129.4 %reduce-scatter.3.cloned.1.call-start = ((), (), s32[]{:S(2)}) async-start(), calls=%async_computation.2 | async-start | bytes 3932160 | tf_op jit(solution)/shard_map/reduce_scatter | solution.py:192
  15.5 29.5 %collective-permute-start = (bf16[256,1024]{1,0:T(8,128)(2,1)S(1)}, bf16[256,1024]{1,0:T(8,128)(2,1)S(1)}, u32[]{:S(2)}, u32[]{:S(2)}) collective-permute-start(bf16[256,1024]{1,0:T(8,128)(2,1)S(1)} %fusion.20), channel_id=1, source_target_pairs={{0,0},{1,4},{2,8},{3,12},{4,1},{5,5},{6,9},{7,13},{8,2},{9,6},{10,... | collective-permute-start | bytes 1572872 | tf_op jit(solution)/shard_map/ppermute | solution.py:176
  45.0 17.2 %copy-start.2 = (bf16[256,1024]{1,0:T(8,128)(2,1)}, bf16[256,1024]{1,0:T(8,128)(2,1)S(1)}, u32[]{:S(2)}) copy-start(bf16[256,1024]{1,0:T(8,128)(2,1)S(1)} %collective-permute-done) | copy-start | bytes 1572868
  45.1 8.6 %collective-permute-start.1 = (bf16[256,1024]{1,0:T(8,128)(2,1)S(1)}, bf16[256,1024]{1,0:T(8,128)(2,1)S(1)}, u32[]{:S(2)}, u32[]{:S(2)}) collective-permute-start(bf16[256,1024]{1,0:T(8,128)(2,1)S(1)} %collective-permute-done), channel_id=1, source_target_pairs={{0,1},{1,2},{2,3},{3,0},{4,5},{5,6},{6,7},{7,4},{8,9},{9,10},{10,1... | collective-permute-start | bytes 1572872 | tf_op jit(solution)/shard_map/ppermute | solution.py:28
  45.1 13.5 %collective-permute-start.3 = (bf16[256,1024]{1,0:T(8,128)(2,1)S(1)}, bf16[256,1024]{1,0:T(8,128)(2,1)S(1)}, u32[]{:S(2)}, u32[]{:S(2)}) collective-permute-start(bf16[256,1024]{1,0:T(8,128)(2,1)S(1)} %collective-permute-done), channel_id=1, source_target_pairs={{1,0},{2,1},{3,2},{0,3},{5,4},{6,5},{7,6},{4,7},{9,8},{10,9},{11,1... | collective-permute-start | bytes 1572872 | tf_op jit(solution)/shard_map/ppermute | solution.py:30
  53.7 8.6 %copy-start.3 = (bf16[256,1024]{1,0:T(8,128)(2,1)}, bf16[256,1024]{1,0:T(8,128)(2,1)S(1)}, u32[]{:S(2)}) copy-start(bf16[256,1024]{1,0:T(8,128)(2,1)S(1)} %collective-permute-done.1) | copy-start | bytes 1572868
  53.7 8.6 %collective-permute-start.2 = (bf16[256,1024]{1,0:T(8,128)(2,1)S(1)}, bf16[256,1024]{1,0:T(8,128)(2,1)S(1)}, u32[]{:S(2)}, u32[]{:S(2)}) collective-permute-start(bf16[256,1024]{1,0:T(8,128)(2,1)S(1)} %collective-permute-done.1), channel_id=1, source_target_pairs={{0,1},{1,2},{2,3},{3,0},{4,5},{5,6},{6,7},{7,4},{8,9},{9,10},{10,1... | collective-permute-start | bytes 1572872 | tf_op jit(solution)/shard_map/ppermute | solution.py:28
  58.6 3.7 %copy-start.4 = (bf16[256,1024]{1,0:T(8,128)(2,1)}, bf16[256,1024]{1,0:T(8,128)(2,1)S(1)}, u32[]{:S(2)}) copy-start(bf16[256,1024]{1,0:T(8,128)(2,1)S(1)} %collective-permute-done.3) | copy-start | bytes 1572868
  62.3 0.8 copy-start.5
  64.8 2.1 copy-start.7
  72.3 0.7 copy-start.1
  72.3 1.3 copy-start.6
  72.3 115.2 %all-gather.2.cloned.1.call-start = ((), (), s32[]{:S(2)}) async-start(), calls=%async_computation.3 | async-start | bytes 1310720 | tf_op jit(solution)/shard_map/all_gather | solution.py:221
  135.9 17.8 %slice-start = ((f32[256,768]{1,0:T(8,128)}), f32[256,512]{1,0:T(8,128)S(1)}, s32[]{:S(2)}) async-start(f32[256,768]{1,0:T(8,128)} %reduce-scatter.3.cloned.1.call-done), calls=%async_computation.5 | async-start | bytes 1048576 | tf_op jit(solution)/shard_map/slice | solution.py:194
  158.0 62.6 %reduce-scatter.5.cloned.1.call-start = ((), (), s32[]{:S(2)}) async-start(), calls=%async_computation.4 | async-start | bytes 2621440 | tf_op jit(solution)/shard_map/reduce_scatter | solution.py:223
  220.6 29.6 %collective-permute-start.4 = (bf16[256,1024]{1,0:T(8,128)(2,1)}, bf16[256,1024]{1,0:T(8,128)(2,1)S(1)}, u32[]{:S(2)}, u32[]{:S(2)}) collective-permute-start(bf16[256,1024]{1,0:T(8,128)(2,1)} %reduce-scatter.5.cloned.1.call-done), channel_id=1, source_target_pairs={{0,0},{1,4},{2,8},{3,12},{4,1},{5,5},{6,9},{7,13},{8,2},{9,6},{10,... | collective-permute-start | bytes 1572872 | tf_op jit(solution)/shard_map/ppermute | solution.py:176
Sparse Core Ops, SparseCore 0:
  72.4 63.4 reduce-scatter.2
  158.1 29.2 all-gather.1
  191.5 29.1 reduce-scatter.4
